TPU v7x, 128 devices: a whole 4x4x4 slice. The times are simulated.
128 devices in a mesh: req: 16 (over z, x), exp: 8 (over y, core).
Axes of the slice: x: 4, y: 4, z: 4, core: 2. Of those that a mesh axis runs over, the one named last changes fastest.
Arguments:
- tokens: bfloat16 [12288, 2880], P(('req', 'exp')), may hold values from -6 to 6
- attn_gain: float32 [2880], replicated, may hold values from 0.5 to 8
- w_query: bfloat16 [2880, 4096], P(None, 'exp'), may hold values from -0.109375 to 0.109375
- key_weight: bfloat16 [2880, 512], P(None, 'exp'), may hold values from -0.109375 to 0.109375
- value_weight: bfloat16 [2880, 512], P(None, 'exp'), may hold values from -0.109375 to 0.109375
- sinks: float32 [64], P('exp'), may hold values from -1 to 3
- w_out: bfloat16 [4096, 2880], P('exp'), may hold values from -0.09375 to 0.09375
- ffn_gain: float32 [2880], replicated, may hold values from 0.25 to 1.75
- router: bfloat16 [2880, 32], replicated, may hold values from -0.109375 to 0.109375
- routes: int32 [12288, 4], P(('req', 'exp')), may hold values from 0 to 31, all different within a row; in each aligned block of 96 rows (0 to 95, 96 to 191, ...) at most 14 rows name the same one
- lengths: int32 [16, 6], P('req'), may hold values from 1 to 384, 768 in all within a row
- expert_gate: bfloat16 [128, 2880, 720], P(('req', 'exp')), may hold values from -0.109375 to 0.109375
- expert_up: bfloat16 [128, 2880, 720], P(('req', 'exp')), may hold values from -0.109375 to 0.109375
- expert_down: bfloat16 [128, 720, 2880], P(('req', 'exp')), may hold values from -0.109375 to 0.109375
Outputs:
- layer_out: bfloat16 [12288, 2880], P(('req', 'exp'))
Inputs may be any that keep to these rules, and one draw needn't show every extreme that they name: `routes`: in the rows of one device no expert is named by more than 14 rows, a bound that some block reaches; a row names 4 different experts.
All inputs are finite; a program needn't handle non-finite values.
Results may differ from a plain program's by a relative error of at most 0.02.
The roundings to bfloat16 on the way count: a program that leaves them out, or rounds other values in their place, can miss the bound.
Values may be sent and summed in bfloat16 or wider, within the bound.
No kernel may reach another device: no remote copies, remote signals or barrier semaphores. Data moves between devices by JAX's collectives and lax.ppermute only.
A program may use at most 192 MiB of HBM per device.

v0:
```python
import jax
import jax.numpy as jnp
from jax import lax
from jax.sharding import PartitionSpec as P

QUERY_HEADS = 64
KEY_VALUE_HEADS = 8
HEAD_DIM = 64
EXPERTS = 32
TOPK = 4
CAP = 14


def rms_norm(value_rows, gain):
    mean_sq = jnp.mean(value_rows * value_rows, axis=-1, keepdims=True)
    return value_rows * lax.rsqrt(mean_sq + 1e-05) * gain


def rotate(value_rows, offset):
    half = value_rows.shape[-1] // 2
    freqs = jnp.exp(
        -(2.0 * jnp.arange(half, dtype=jnp.float32) / value_rows.shape[-1])
        * jnp.log(jnp.float32(150000.0))
    )
    angle = offset.astype(jnp.float32)[:, None] * freqs[None, :]
    cosine = jnp.cos(angle)[:, None, :]
    sine = jnp.sin(angle)[:, None, :]
    first = value_rows[..., :half]
    second = value_rows[..., half:]
    return jnp.concatenate(
        [first * cosine - second * sine, second * cosine + first * sine], axis=-1
    )


def per_device(
    tokens,
    attn_gain,
    w_query,
    key_weight,
    value_weight,
    sinks,
    w_out,
    ffn_gain,
    router,
    routes,
    lengths,
    expert_gate,
    expert_up,
    expert_down,
):
    tok_rows = tokens.shape[0]
    model_width = tokens.shape[1]
    local_heads = w_query.shape[1] // HEAD_DIM
    local_kv = key_weight.shape[1] // HEAD_DIM
    head_group = QUERY_HEADS // KEY_VALUE_HEADS
    normed_input = rms_norm(tokens.astype(jnp.float32), attn_gain).astype(jnp.bfloat16)
    by_chip = lax.all_gather(normed_input, "y", axis=0, tiled=False)
    piece = lax.all_gather(by_chip, "c", axis=1, tiled=True).reshape(-1, model_width)
    projected = jnp.concatenate(
        [
            jnp.dot(piece, w_query, preferred_element_type=jnp.float32),
            jnp.dot(piece, key_weight, preferred_element_type=jnp.float32),
            jnp.dot(piece, value_weight, preferred_element_type=jnp.float32),
        ],
        axis=1,
    )
    item_count = projected.shape[0]
    lens = lengths[0]
    ends = jnp.cumsum(lens)
    starts = ends - lens
    position = jnp.arange(item_count, dtype=jnp.int32)
    member = ((position[:, None] >= starts[None, :]) & (position[:, None] < ends[None, :])).astype(
        jnp.int32
    )
    segment = jnp.sum(member * jnp.arange(lens.shape[0], dtype=jnp.int32)[None, :], axis=1)
    offset = position - jnp.sum(member * starts[None, :], axis=1)
    q_width = local_heads * HEAD_DIM
    kv_width = local_kv * HEAD_DIM
    query_rows = rotate(
        projected[:, :q_width].reshape(item_count, local_heads, HEAD_DIM), offset
    ).astype(jnp.bfloat16)
    key_rows = rotate(
        projected[:, q_width : q_width + kv_width].reshape(item_count, local_kv, HEAD_DIM), offset
    ).astype(jnp.bfloat16)
    value_rows = (
        projected[:, q_width + kv_width :]
        .reshape(item_count, local_kv, HEAD_DIM)
        .astype(jnp.bfloat16)
    )
    grouped_heads = query_rows.reshape(item_count, local_kv, head_group, HEAD_DIM)
    scores = jnp.einsum(
        "qcgd,kcd->cgqk", grouped_heads, key_rows, preferred_element_type=jnp.float32
    ) * HEAD_DIM ** (-0.5)
    allowed = (segment[:, None] == segment[None, :]) & (position[None, :] <= position[:, None])
    sink_score_logit = sinks.reshape(local_kv, head_group, 1, 1)
    masked = jnp.where(allowed[None, None], scores, -jnp.inf)
    top = jnp.maximum(jnp.max(masked, axis=-1, keepdims=True), sink_score_logit)
    expo = jnp.where(allowed[None, None], jnp.exp(scores - top), 0.0)
    denom = jnp.sum(expo, axis=-1, keepdims=True) + jnp.exp(sink_score_logit - top)
    probs = (expo / denom).astype(jnp.bfloat16)
    attended = jnp.einsum("cgqk,kcd->qcgd", probs, value_rows, preferred_element_type=jnp.float32)
    attended = attended.reshape(item_count, q_width).astype(jnp.bfloat16)
    head_term = jnp.dot(attended, w_out, preferred_element_type=jnp.float32).astype(jnp.bfloat16)
    n_y = lax.axis_size("y")
    n_c = lax.axis_size("c")
    head_term = head_term.reshape(n_y, n_c, tok_rows, model_width).transpose(1, 0, 2, 3)
    on_chip = lax.psum_scatter(head_term, "c", scatter_dimension=0, tiled=True)
    attn_sum = (
        lax.psum_scatter(
            on_chip.reshape(n_y, tok_rows, model_width), "y", scatter_dimension=0, tiled=True
        )
        .reshape(tok_rows, model_width)
        .astype(jnp.float32)
    )
    residual = (tokens.astype(jnp.float32) + attn_sum).astype(jnp.bfloat16)
    normed2 = rms_norm(residual.astype(jnp.float32), ffn_gain).astype(jnp.bfloat16)
    logits = jnp.dot(normed2, router, preferred_element_type=jnp.float32)
    picked = jnp.take_along_axis(logits, routes, axis=1)
    weights = jax.nn.softmax(picked, axis=-1)
    flat_routes = routes.reshape(-1)
    expert_ids = jnp.arange(EXPERTS, dtype=jnp.int32)
    onehot_route = (flat_routes[:, None] == expert_ids[None, :]).astype(jnp.int32)
    rank = jnp.cumsum(onehot_route, axis=0) - 1
    slot_rank = jnp.sum(onehot_route * rank, axis=1)
    flat_slot = flat_routes * CAP + slot_rank
    slot_ids = jnp.arange(EXPERTS * CAP, dtype=jnp.int32)
    dispatch_table = (slot_ids[:, None] == flat_slot[None, :]).astype(jnp.bfloat16)
    repeated = jnp.repeat(normed2, TOPK, axis=0)
    packed = jnp.dot(dispatch_table, repeated, preferred_element_type=jnp.float32).astype(
        jnp.bfloat16
    )
    halves = n_y // (EXPERTS // lax.axis_size("req"))
    send_rows = jnp.broadcast_to(
        packed.reshape(EXPERTS, 1, CAP, model_width), (EXPERTS, halves, CAP, model_width)
    ).reshape(EXPERTS * halves, CAP, model_width)
    received = lax.all_to_all(send_rows, ("req", "y"), split_axis=0, concat_axis=0, tiled=True)
    both = lax.all_gather(received, "c", axis=0, tiled=False)
    flat_rows = both.reshape(-1, model_width)
    gate = jnp.dot(flat_rows, expert_gate[0], preferred_element_type=jnp.float32)
    up_val = jnp.dot(flat_rows, expert_up[0], preferred_element_type=jnp.float32)
    hidden = ((up_val + 1.0) * gate * jax.nn.sigmoid(1.702 * gate)).astype(jnp.bfloat16)
    slice_out = jnp.dot(hidden, expert_down[0], preferred_element_type=jnp.float32).astype(
        jnp.bfloat16
    )
    swapped = lax.all_to_all(
        slice_out.reshape(both.shape), "c", split_axis=0, concat_axis=0, tiled=True
    )
    chip_sum = swapped.astype(jnp.float32).sum(axis=0).astype(jnp.bfloat16)
    returned = lax.all_to_all(chip_sum, ("req", "y"), split_axis=0, concat_axis=0, tiled=True)
    summed = returned.astype(jnp.float32).reshape(EXPERTS, halves, CAP, model_width).sum(axis=1)
    summed = summed.reshape(EXPERTS * CAP, model_width)
    picked_rows = jnp.take(summed, flat_slot, axis=0).reshape(tok_rows, TOPK, model_width)
    moe_sum = jnp.sum(weights[:, :, None] * picked_rows, axis=1)
    return (residual.astype(jnp.float32) + moe_sum).astype(jnp.bfloat16)


def solution(mesh):
    n_req, n_exp = mesh.devices.shape
    fine = jax.sharding.Mesh(mesh.devices.reshape(n_req, n_exp // 2, 2), ("req", "y", "c"))
    tok = ("req", "y", "c")
    return jax.shard_map(
        per_device,
        mesh=fine,
        in_specs=(
            P(tok, None),
            P(),
            P(None, ("y", "c")),
            P(None, ("y", "c")),
            P(None, ("y", "c")),
            P(("y", "c")),
            P(("y", "c"), None),
            P(),
            P(),
            P(tok, None),
            P("req", None),
            P(tok, None, None),
            P(tok, None, None),
            P(tok, None, None),
        ),
        out_specs=P(tok, None),
        check_vma=False,
    )
```

profile of v0, /device:TPU:10, one launch (start us, length us, event | category | flops | bytes accessed | tf_op | source)
XLA Modules:
  0.0 604.9 jit_solution(8165540641719783037)
XLA Ops:
  10.1 33.6 %all-gather.8.cloned.1.call-done = bf16[384,2880]{1,0:T(8,128)(2,1)} async-done(((bf16[96,2880]{1,0:T(8,128)(2,1)}), bf16[384,2880]{1,0:T(8,128)(2,1)}) %all-gather.8.cloned.1.call-update) | async-done | bytes 2211856 | tf_op jit(solution)/shard_map/all_gather | solution.py:57
  50.2 13.1 %all-gather.6.cloned.1.call-done = bf16[4,192,2880]{2,1,0:T(8,128)(2,1)} async-done(((bf16[4,96,2880]{2,1,0:T(8,128)(2,1)}), bf16[4,192,2880]{2,1,0:T(8,128)(2,1)}) %all-gather.6.cloned.1.call-update) | async-done | bytes 4423696 | tf_op jit(solution)/shard_map/all_gather | solution.py:58
  72.5 8.1 %fusion = (f32[8,768]{1,0:T(8,128)S(1)}, f32[768,768,8]{1,0,2:T(8,128)}) fusion(pred[768,768]{0,1:T(8,128)(4,1)S(1)} %fusion.13, bf16[768,8,32]{0,2,1:T(8,128)(2,1)S(1)} %get-tuple-element.10, bf16[768,8,32]{0,2,1:T(8,128)(2,1)S(1)} %get-tuple-element.9, bf16[768,32]{0,1:T(8,128)(2,1)S(1)} %get-tuple-element.12, bf16[768,32]{0,1:T(8,128)(2,1)S(1)} %get-tuple-element.11), kind=kOutput, calls=%fused_computation.4 | convolution fusion | flops 619898880 | bytes 20373504 | tf_op jit(solution)/shard_map/qcgd,kcd->cgqk/dot_general | solution.py:91
  82.0 10.8 %fusion.3 = f32[8,768]{1,0:T(8,128)} fusion(f32[768,768,8]{1,0,2:T(8,128)} %get-tuple-element.16, f32[8,768]{1,0:T(8,128)} %broadcast_maximum_fusion, pred[768,768]{0,1:T(8,128)(4,1)S(1)} %fusion.13), kind=kLoop, calls=%fused_computation.8 | loop fusion | flops 18868224 | bytes 19513344 | tf_op jit(solution)/shard_map/reduce_sum | solution.py:99
  94.2 14.4 %fusion.16 = bf16[64,8,768]{2,0,1:T(8,128)(2,1)} fusion(f32[8,768]{1,0:T(8,128)} %exponential_add_fusion, f32[8,768]{1,0:T(8,128)} %broadcast_maximum_fusion, f32[768,768,8]{1,0,2:T(8,128)} %get-tuple-element.16, pred[768,768]{0,1:T(8,128)(4,1)S(1)} %fusion.13, bf16[768,2880]{1,0:T(8,128)(2,1)} %bitcast.132, bf16[2880,64]{0,1:T(8,128)(2,1)} %param.18), kind=kOutput, calls=%fused_computation.31 | convolution fusion | flops 911130624 | bytes 25092096 | tf_op jit(solution)/shard_map/cgqk,kcd->qcgd/dot_general | solution.py:101
  114.2 6.6 %copy.112 = bf16[768,2880]{1,0:T(8,128)(2,1)} copy(bf16[768,2880]{0,1:T(8,128)(2,1)} %convolution_convert_fusion.1) | data formatting | bytes 8847360 | tf_op jit(solution)/shard_map/convert_element_type | solution.py:103
  121.5 35.2 %all-reduce.3.cloned.1.call-done = bf16[2,4,96,2880]{3,2,0,1:T(8,128)(2,1)} async-done(((bf16[2,4,96,2880]{3,2,0,1:T(8,128)(2,1)}), bf16[2,4,96,2880]{3,2,0,1:T(8,128)(2,1)}) %all-reduce.3.cloned.1.call-update) | async-done | bytes 4423696
  162.3 29.5 %reduce-scatter.3.cloned.1.call-done = bf16[1,96,2880]{2,1,0:T(8,128)(2,1)} async-done(((bf16[4,96,2880]{2,1,0:T(8,128)(2,1)}), bf16[1,96,2880]{2,1,0:T(8,128)(2,1)}) %reduce-scatter.3.cloned.1.call-update) | async-done | bytes 552976 | tf_op jit(solution)/shard_map/reduce_scatter | solution.py:109
  208.8 92.3 %all_to_all.15 = bf16[64,14,2880]{2,1,0:T(8,128)(2,1)S(1)} all-to-all(bf16[64,14,2880]{2,1,0:T(8,128)(2,1)S(1)} %bitcast.129), channel_id=1, replica_groups=mesh['req'=16,'y'=4,'c'=2] {'req','y'}, dimensions={0} | all-to-all | bytes 10321920 | tf_op jit(solution)/shard_map/all_to_all | solution.py:136
  304.7 23.4 %all-gather.10.cloned.1.call-done = bf16[128,14,2880]{2,0,1:T(8,128)(2,1)} async-done(((bf16[64,14,2880]{2,0,1:T(8,128)(2,1)}), bf16[128,14,2880]{2,0,1:T(8,128)(2,1)}) %all-gather.10.cloned.1.call-update) | async-done | bytes 10321936 | tf_op jit(solution)/shard_map/all_gather | solution.py:137
  328.1 13.6 %copy.122 = bf16[128,14,2880]{2,1,0:T(8,128)(2,1)} copy(bf16[128,14,2880]{2,0,1:T(8,128)(2,1)} %all-gather.10.cloned.1.call-done) | data formatting | bytes 20643840 | tf_op jit(solution)/shard_map/all_gather | solution.py:137
  341.7 15.4 %reshape.432 = bf16[1792,2880]{1,0:T(8,128)(2,1)} reshape(bf16[128,14,2880]{2,1,0:T(8,128)(2,1)} %copy.122) | data formatting | bytes 20643840 | tf_op jit(solution)/shard_map/reshape | solution.py:138
  357.1 14.6 %fusion.7 = f32[1792,720]{0,1:T(8,128)} fusion(bf16[1792,2880]{1,0:T(8,128)(2,1)} %reshape.432, bf16[1,2880,720]{1,2,0:T(8,128)(2,1)} %param.25), kind=kOutput, calls=%fused_computation.18 | convolution fusion | flops 7431782400 | bytes 19630080 | tf_op jit(solution)/shard_map/dot_general | solution.py:139
  371.7 27.3 %convolution_convert_fusion = bf16[1792,2880]{0,1:T(8,128)(2,1)} fusion(bf16[1,720,2880]{2,1,0:T(8,128)(2,1)} %param.27, f32[1792,720]{0,1:T(8,128)} %fusion.7, bf16[1792,2880]{1,0:T(8,128)(2,1)} %reshape.432, bf16[1,2880,720]{1,2,0:T(8,128)(2,1)} %param.26), kind=kOutput, calls=%fused_computation.10 | convolution fusion | flops 14879047680 | bytes 34099200 | tf_op jit(solution)/shard_map/dot_general | solution.py:142
  399.0 14.5 %copy.123 = bf16[1792,2880]{1,0:T(8,128)(2,1)} copy(bf16[1792,2880]{0,1:T(8,128)(2,1)} %convolution_convert_fusion) | data formatting | bytes 20643840 | tf_op jit(solution)/shard_map/convert_element_type | solution.py:142
  413.4 14.4 %reshape.433 = bf16[2,64,14,2880]{3,2,1,0:T(8,128)(2,1)} reshape(bf16[1792,2880]{1,0:T(8,128)(2,1)} %copy.123) | data formatting | bytes 20643840 | tf_op jit(solution)/shard_map/reshape | solution.py:146
  427.8 10.7 %copy.124 = bf16[2,64,14,2880]{3,1,2,0:T(8,128)(2,1)S(1)} copy(bf16[2,64,14,2880]{3,2,1,0:T(8,128)(2,1)} %reshape.433) | data formatting | bytes 20643840 | tf_op jit(solution)/shard_map/reshape | solution.py:146
  438.5 14.0 %all_to_all.16 = bf16[2,64,14,2880]{3,1,2,0:T(8,128)(2,1)} all-to-all(bf16[2,64,14,2880]{3,1,2,0:T(8,128)(2,1)S(1)} %copy.124), channel_id=1, replica_groups=mesh['req'=16,'y'=4,'c'=2] {'c'}, dimensions={0} | all-to-all | bytes 20643840 | tf_op jit(solution)/shard_map/all_to_all | solution.py:145
  452.5 9.7 %reduce_sum.105 = bf16[64,14,2880]{2,0,1:T(8,128)(2,1)} reduce(bf16[2,64,14,2880]{3,1,2,0:T(8,128)(2,1)} %all_to_all.16, bf16[]{:T(256)} %constant.70.clone.1), dimensions={0}, to_apply=%region_14.15 | reduce | flops 2580480 | bytes 15482882 | tf_op jit(solution)/shard_map/reduce_sum | solution.py:148
  462.1 8.0 %copy.125 = bf16[64,14,2880]{2,1,0:T(8,128)(2,1)} copy(bf16[64,14,2880]{2,0,1:T(8,128)(2,1)} %reduce_sum.105) | data formatting | bytes 10321920 | tf_op jit(solution)/shard_map/reduce_sum | solution.py:148
  470.1 11.1 %all-to-all-start.2 = ((bf16[64,14,2880]{2,1,0:T(8,128)(2,1)}), bf16[64,14,2880]{2,1,0:T(8,128)(2,1)}, u32[]{:S(2)}, u32[]{:S(2)}) async-start(bf16[64,14,2880]{2,1,0:T(8,128)(2,1)} %copy.125), calls=%async_computation.3 | async-start | bytes 12058624 | tf_op jit(solution)/shard_map/all_to_all | solution.py:149
  486.2 76.9 %all-to-all-done.2 = bf16[64,14,2880]{2,1,0:T(8,128)(2,1)} async-done(((bf16[64,14,2880]{2,1,0:T(8,128)(2,1)}), bf16[64,14,2880]{2,1,0:T(8,128)(2,1)}, u32[]{:S(2)}, u32[]{:S(2)}) %all-to-all-start.2) | async-done | bytes 5160992 | tf_op jit(solution)/shard_map/all_to_all | solution.py:149
  563.1 7.0 %convert_reduce_fusion = f32[32,14,2880]{2,1,0:T(8,128)} fusion(bf16[64,14,2880]{2,1,0:T(8,128)(2,1)} %all-to-all-done.2), kind=kLoop, calls=%fused_computation.9 | loop fusion | flops 3870720 | bytes 10321920 | tf_op jit(solution)/shard_map/reduce_sum | solution.py:150
  575.8 9.0 %gather_fusion = f32[384,2880]{1,0:T(8,128)} fusion(f32[448,2880]{1,0:T(8,128)} %reshape.436, s32[1024]{0:T(1024)S(1)} %pad_clamp_fusion), kind=kCustom, calls=%fused_computation | custom fusion | bytes 8848896 | tf_op jit(solution)/shard_map/jit(_take)/gather | solution.py:152
  (100 shorter events, 77.7 us)
Async XLA Ops:
  6.5 102.1 %copy-start = (bf16[512,2880]{0,1:T(8,128)(2,1)S(1)}, bf16[512,2880]{0,1:T(8,128)(2,1)}, u32[]{:S(2)}) copy-start(bf16[512,2880]{0,1:T(8,128)(2,1)} %param.20) | copy-start | bytes 8847364
  6.5 37.2 %all-gather.8.cloned.1.call-start = ((), (), s32[]{:S(2)}) async-start(), calls=%async_computation.6 | async-start | bytes 2826240 | tf_op jit(solution)/shard_map/all_gather | solution.py:57
  10.0 38.4 %copy-start.12 = (s32[1,6]{1,0:T(1,128)S(1)}, s32[1,6]{1,0:T(1,128)}, u32[]{:S(2)}) copy-start(s32[1,6]{1,0:T(1,128)} %param.24) | copy-start | bytes 76
  10.1 53.3 %all-gather.6.cloned.1.call-start = ((), (), s32[]{:S(2)}) async-start(), calls=%async_computation.4 | async-start | bytes 6782976 | tf_op jit(solution)/shard_map/all_gather | solution.py:58
  43.8 112.9 %all-reduce.3.cloned.1.call-start = ((), (), s32[]{:S(2)}) async-start(), calls=%async_computation.8 | async-start | bytes 9043968
  63.4 4.4 copy-start.4
  67.7 4.6 copy-start.5
  67.7 4.6 copy-start.6
  72.5 8.8 %copy-start.11 = (f32[8]{0:T(128)S(1)}, f32[8]{0:T(128)}, u32[]{:S(2)}) copy-start(f32[8]{0:T(128)} %param.19) | copy-start | bytes 100
  80.7 0.6 copy-start.7
  114.2 6.7 %copy-start.13 = (u32[128]{0:T(128)S(1)}, u32[128]{0:T(128)}, u32[]{:S(2)}) copy-start(u32[128]{0:T(128)} %constant.92) | copy-start | bytes 1540
  120.8 39.8 %copy-start.9 = (s32[96,4]{0,1:T(4,128)S(1)}, s32[96,4]{0,1:T(4,128)}, u32[]{:S(2)}) copy-start(s32[96,4]{0,1:T(4,128)} %param.23) | copy-start | bytes 4612
  120.8 71.0 %copy-start.2 = (bf16[96,2880]{1,0:T(8,128)(2,1)S(1)}, bf16[96,2880]{1,0:T(8,128)(2,1)}, u32[]{:S(2)}) copy-start(bf16[96,2880]{1,0:T(8,128)(2,1)} %param.14) | copy-start | bytes 1658884
  120.8 72.3 %copy-start.10 = (f32[2880]{0:T(1024)S(1)}, f32[2880]{0:T(1024)}, u32[]{:S(2)}) copy-start(f32[2880]{0:T(1024)} %param.21) | copy-start | bytes 34564
  120.9 70.9 %reduce-scatter.3.cloned.1.call-start = ((), (), s32[]{:S(2)}) async-start(), calls=%async_computation.5 | async-start | bytes 2826240 | tf_op jit(solution)/shard_map/reduce_scatter | solution.py:109
  160.6 167.5 %all-gather.10.cloned.1.call-start = ((), (), s32[]{:S(2)}) async-start(), calls=%async_computation.7 | async-start | bytes 15826944 | tf_op jit(solution)/shard_map/all_gather | solution.py:137
  470.1 11.9 %copy-start.8 = (bf16[2880,32]{0,1:T(8,128)(2,1)S(1)}, bf16[2880,32]{0,1:T(8,128)(2,1)}, u32[]{:S(2)}) copy-start(bf16[2880,32]{0,1:T(8,128)(2,1)} %param.22) | copy-start | bytes 552964
  470.1 93.0 %all-to-all-start.2 = ((bf16[64,14,2880]{2,1,0:T(8,128)(2,1)}), bf16[64,14,2880]{2,1,0:T(8,128)(2,1)}, u32[]{:S(2)}, u32[]{:S(2)}) async-start(bf16[64,14,2880]{2,1,0:T(8,128)(2,1)} %copy.125), calls=%async_computation.3 | async-start | bytes 12058624 | tf_op jit(solution)/shard_map/all_to_all | solution.py:149
  584.8 13.1 %copy-start.1 = (bf16[512,2880]{0,1:T(8,128)(2,1)S(1)}, bf16[512,2880]{0,1:T(8,128)(2,1)}, u32[]{:S(2)}) copy-start(bf16[512,2880]{0,1:T(8,128)(2,1)} %param.20) | copy-start | bytes 8847364
  590.4 6.5 %copy-start.3 = (bf16[1,96,2880]{2,1,0:T(8,128)(2,1)S(1)}, bf16[1,96,2880]{2,1,0:T(8,128)(2,1)}, u32[]{:S(2)}) copy-start(bf16[1,96,2880]{2,1,0:T(8,128)(2,1)} %reduce-scatter.3.cloned.1.call-done) | copy-start | bytes 1658884
Sparse Core Ops, SparseCore 0:
  10.2 33.5 all-gather.7
  45.4 17.8 all-gather.5
  120.9 35.7 all-reduce.2
  160.7 31.0 reduce-scatter.2
  304.8 23.2 all-gather.9
where the time goes:
time: 614 us; the launch traced here: 605 us
  waiting for transfers between devices  212 us (35%)
  local copies, waits for them, and re-layouts  131 us (21%)
  blocking collectives  106 us (17%)
  matrix products  83.4 us (14%)
  other arithmetic  46.8 us (8%)
  between operations  13.9 us (2%)
  starting transfers between devices  11.3 us (2%)
    all_to_all x1, blocking collectives, per_device(): lax.all_to_all(send_rows, ('req', 'y'), split_axis=0, concat_axis=0, tile...  92.3 us
    all_to_all x1, waiting for transfers between devices, per_device(): lax.all_to_all(chip_sum, ('req', 'y'), split_axis=0, concat_axis=0, tiled...  76.9 us
    unnamed x6, waiting for transfers between devices  35.3 us
    all_gather x1, waiting for transfers between devices, per_device(): by_chip = lax.all_gather(normed_input, 'y', axis=0, tiled=False)  33.6 us
    reduce_scatter x1, waiting for transfers between devices, per_device(): lax.psum_scatter(on_chip.reshape(n_y, tok_rows, model_width), 'y', scatte...  29.5 us
    dot_general x1, matrix products, per_device(): jnp.dot(hidden, expert_down[0], preferred_element_type=jnp.float32)  27.3 us
    reshape x2, local copies, waits for them, and re-layouts, per_device(): slice_out.reshape(both.shape)  25.1 us
    all_gather x1, waiting for transfers between devices, per_device(): both = lax.all_gather(received, 'c', axis=0, tiled=False)  23.4 us
  transfers between devices with their start and end apart: 6, of which 6 were waited for; matrix products, arithmetic and copies ran while one was open for 2% of the time, Pallas kernels for 0%

commit v1 on v0

--- a/solution.py
+++ b/solution.py
@@ -9,6 +9,13 @@
 EXPERTS = 32
 TOPK = 4
 CAP = 14
+
+
+def all_by_exchange(block, axis, dim):
+    peers = lax.axis_size(axis)
+    pieces = jnp.stack([block for _ in range(peers)])
+    pieces = lax.all_to_all(pieces, axis, split_axis=0, concat_axis=0)
+    return jnp.concatenate(pieces, axis=dim)
 
 
 def rms_norm(value_rows, gain):
@@ -55,7 +62,7 @@
     head_group = QUERY_HEADS // KEY_VALUE_HEADS
     normed_input = rms_norm(tokens.astype(jnp.float32), attn_gain).astype(jnp.bfloat16)
     by_chip = lax.all_gather(normed_input, "y", axis=0, tiled=False)
-    piece = lax.all_gather(by_chip, "c", axis=1, tiled=True).reshape(-1, model_width)
+    piece = all_by_exchange(by_chip, "c", 1).reshape(-1, model_width)
     projected = jnp.concatenate(
         [
             jnp.dot(piece, w_query, preferred_element_type=jnp.float32),

time: 614 us -> 586 us (0.954)
  waiting for transfers between devices: 212 us -> 193 us
    all_gather x1 -> x0, waiting for transfers between devices: 13.1 us -> none  [per_device(): lax.all_gather(by_chip, 'c', axis=1, tiled=True).reshape(-1, model_width)]
    all_to_all x1, blocking collectives: 92.3 us -> 80.2 us  [per_device(): lax.all_to_all(send_rows, ('req', 'y'), split_axis=0, concat_axis=0, tile...]
    all_to_all x0 -> x1, blocking collectives: none -> 7.52 us  [all_by_exchange(): pieces = lax.all_to_all(pieces, axis, split_axis=0, concat_axis=0)]
    all_gather x1, waiting for transfers between devices: 33.6 us -> 27.3 us  [per_device(): by_chip = lax.all_gather(normed_input, 'y', axis=0, tiled=False)]
    unnamed x6 -> x5, waiting for transfers between devices: 35.3 us -> 35 us
  transfers between devices with their start and end apart: 6 -> 5, of which waited for: 6 -> 5; matrix products, arithmetic and copies ran while one was open for 2% -> 2% of each run, Pallas kernels for 0% -> 0%
where the time goes in v1:
time: 586 us; the launch traced here: 582 us
  waiting for transfers between devices  193 us (33%)
  local copies, waits for them, and re-layouts  133 us (23%)
  blocking collectives  102 us (17%)
  matrix products  79.3 us (14%)
  other arithmetic  49.6 us (8%)
  between operations  13.7 us (2%)
  starting transfers between devices  11.2 us (2%)
    all_to_all x1, blocking collectives, per_device(): lax.all_to_all(send_rows, ('req', 'y'), split_axis=0, concat_axis=0, tile...  80.2 us
    all_to_all x1, waiting for transfers between devices, per_device(): lax.all_to_all(chip_sum, ('req', 'y'), split_axis=0, concat_axis=0, tiled...  76.9 us
    unnamed x5, waiting for transfers between devices  35 us
    reduce_scatter x1, waiting for transfers between devices, per_device(): lax.psum_scatter(on_chip.reshape(n_y, tok_rows, model_width), 'y', scatte...  29.5 us
    dot_general x1, matrix products, per_device(): jnp.dot(hidden, expert_down[0], preferred_element_type=jnp.float32)  27.7 us
    all_gather x1, waiting for transfers between devices, per_device(): by_chip = lax.all_gather(normed_input, 'y', axis=0, tiled=False)  27.3 us
    reshape x2, local copies, waits for them, and re-layouts, per_device(): slice_out.reshape(both.shape)  25.1 us
    all_gather x1, waiting for transfers between devices, per_device(): both = lax.all_gather(received, 'c', axis=0, tiled=False)  24.2 us
  transfers between devices with their start and end apart: 5, of which 5 were waited for; matrix products, arithmetic and copies ran while one was open for 2% of the time, Pallas kernels for 0%

profile of v1, /device:TPU:10, one launch (start us, length us, event | category | flops | bytes accessed | tf_op | source)
XLA Modules:
  0.0 581.6 jit_solution(6751072774722703746)
XLA Ops:
  16.5 27.3 %all-gather.5.cloned.1.call-done = bf16[384,2880]{1,0:T(8,128)(2,1)} async-done(((bf16[96,2880]{1,0:T(8,128)(2,1)}), bf16[384,2880]{1,0:T(8,128)(2,1)}) %all-gather.5.cloned.1.call-update) | async-done | bytes 2211856 | tf_op jit(solution)/shard_map/all_gather | solution.py:64
  46.6 7.5 %all_to_all.20 = bf16[2,4,96,2880]{3,2,1,0:T(8,128)(2,1)S(1)} all-to-all(bf16[2,4,96,2880]{3,2,1,0:T(8,128)(2,1)S(1)} %pad_maximum_fusion), channel_id=1, replica_groups=mesh['req'=16,'y'=4,'c'=2] {'c'}, dimensions={0} | all-to-all | bytes 8847360 | tf_op jit(solution)/shard_map/all_to_all | solution.py:17
  60.9 8.1 %fusion = (f32[8,768]{1,0:T(8,128)S(1)}, f32[768,768,8]{1,0,2:T(8,128)}) fusion(pred[768,768]{0,1:T(8,128)(4,1)S(1)} %fusion.13, bf16[768,8,32]{0,2,1:T(8,128)(2,1)S(1)} %get-tuple-element.10, bf16[768,8,32]{0,2,1:T(8,128)(2,1)S(1)} %get-tuple-element.9, bf16[768,32]{0,1:T(8,128)(2,1)S(1)} %get-tuple-element.12, bf16[768,32]{0,1:T(8,128)(2,1)S(1)} %get-tuple-element.11), kind=kOutput, calls=%fused_computation.4 | convolution fusion | flops 619898880 | bytes 20373504 | tf_op jit(solution)/shard_map/qcgd,kcd->cgqk/dot_general | solution.py:98
  70.3 10.8 %fusion.3 = f32[8,768]{1,0:T(8,128)} fusion(f32[768,768,8]{1,0,2:T(8,128)} %get-tuple-element.16, f32[8,768]{1,0:T(8,128)} %broadcast_maximum_fusion, pred[768,768]{0,1:T(8,128)(4,1)S(1)} %fusion.13), kind=kLoop, calls=%fused_computation.8 | loop fusion | flops 18868224 | bytes 19513344 | tf_op jit(solution)/shard_map/reduce_sum | solution.py:106
  82.5 14.3 %fusion.16 = bf16[64,8,768]{2,0,1:T(8,128)(2,1)} fusion(f32[8,768]{1,0:T(8,128)} %exponential_add_fusion, f32[8,768]{1,0:T(8,128)} %broadcast_maximum_fusion, f32[768,768,8]{1,0,2:T(8,128)} %get-tuple-element.16, pred[768,768]{0,1:T(8,128)(4,1)S(1)} %fusion.13, bf16[768,2880]{1,0:T(8,128)(2,1)} %bitcast.133, bf16[2880,64]{0,1:T(8,128)(2,1)} %param.18), kind=kOutput, calls=%fused_computation.32 | convolution fusion | flops 911130624 | bytes 25092096 | tf_op jit(solution)/shard_map/cgqk,kcd->qcgd/dot_general | solution.py:108
  102.5 6.6 %copy.120 = bf16[768,2880]{1,0:T(8,128)(2,1)} copy(bf16[768,2880]{0,1:T(8,128)(2,1)} %convolution_convert_fusion.1) | data formatting | bytes 8847360 | tf_op jit(solution)/shard_map/convert_element_type | solution.py:110
  109.8 34.9 %all-reduce.3.cloned.1.call-done = bf16[2,4,96,2880]{3,2,0,1:T(8,128)(2,1)} async-done(((bf16[2,4,96,2880]{3,2,0,1:T(8,128)(2,1)}), bf16[2,4,96,2880]{3,2,0,1:T(8,128)(2,1)}) %all-reduce.3.cloned.1.call-update) | async-done | bytes 4423696
  150.3 29.5 %reduce-scatter.3.cloned.1.call-done = bf16[1,96,2880]{2,1,0:T(8,128)(2,1)} async-done(((bf16[4,96,2880]{2,1,0:T(8,128)(2,1)}), bf16[1,96,2880]{2,1,0:T(8,128)(2,1)}) %reduce-scatter.3.cloned.1.call-update) | async-done | bytes 552976 | tf_op jit(solution)/shard_map/reduce_scatter | solution.py:116
  196.9 80.2 %all_to_all.21 = bf16[64,14,2880]{2,1,0:T(8,128)(2,1)S(1)} all-to-all(bf16[64,14,2880]{2,1,0:T(8,128)(2,1)S(1)} %bitcast.130), channel_id=1, replica_groups=mesh['req'=16,'y'=4,'c'=2] {'req','y'}, dimensions={0} | all-to-all | bytes 10321920 | tf_op jit(solution)/shard_map/all_to_all | solution.py:143
  280.5 24.2 %all-gather.7.cloned.1.call-done = bf16[128,14,2880]{2,0,1:T(8,128)(2,1)} async-done(((bf16[64,14,2880]{2,0,1:T(8,128)(2,1)}), bf16[128,14,2880]{2,0,1:T(8,128)(2,1)}) %all-gather.7.cloned.1.call-update) | async-done | bytes 10321936 | tf_op jit(solution)/shard_map/all_gather | solution.py:144
  304.7 13.6 %copy.130 = bf16[128,14,2880]{2,1,0:T(8,128)(2,1)} copy(bf16[128,14,2880]{2,0,1:T(8,128)(2,1)} %all-gather.7.cloned.1.call-done) | data formatting | bytes 20643840 | tf_op jit(solution)/shard_map/all_gather | solution.py:144
  318.3 15.4 %reshape.432 = bf16[1792,2880]{1,0:T(8,128)(2,1)} reshape(bf16[128,14,2880]{2,1,0:T(8,128)(2,1)} %copy.130) | data formatting | bytes 20643840 | tf_op jit(solution)/shard_map/reshape | solution.py:145
  333.7 14.6 %fusion.7 = f32[1792,720]{0,1:T(8,128)} fusion(bf16[1792,2880]{1,0:T(8,128)(2,1)} %reshape.432, bf16[1,2880,720]{1,2,0:T(8,128)(2,1)} %param.25), kind=kOutput, calls=%fused_computation.19 | convolution fusion | flops 7431782400 | bytes 19630080 | tf_op jit(solution)/shard_map/dot_general | solution.py:146
  348.3 27.7 %convolution_convert_fusion = bf16[1792,2880]{0,1:T(8,128)(2,1)} fusion(bf16[1,720,2880]{2,1,0:T(8,128)(2,1)} %param.27, f32[1792,720]{0,1:T(8,128)} %fusion.7, bf16[1792,2880]{1,0:T(8,128)(2,1)} %reshape.432, bf16[1,2880,720]{1,2,0:T(8,128)(2,1)} %param.26), kind=kOutput, calls=%fused_computation.10 | convolution fusion | flops 14879047680 | bytes 34099200 | tf_op jit(solution)/shard_map/dot_general | solution.py:149
  376.0 14.5 %copy.131 = bf16[1792,2880]{1,0:T(8,128)(2,1)} copy(bf16[1792,2880]{0,1:T(8,128)(2,1)} %convolution_convert_fusion) | data formatting | bytes 20643840 | tf_op jit(solution)/shard_map/convert_element_type | solution.py:149
  390.5 14.4 %reshape.433 = bf16[2,64,14,2880]{3,2,1,0:T(8,128)(2,1)} reshape(bf16[1792,2880]{1,0:T(8,128)(2,1)} %copy.131) | data formatting | bytes 20643840 | tf_op jit(solution)/shard_map/reshape | solution.py:153
  404.9 10.7 %copy.132 = bf16[2,64,14,2880]{3,1,2,0:T(8,128)(2,1)S(1)} copy(bf16[2,64,14,2880]{3,2,1,0:T(8,128)(2,1)} %reshape.433) | data formatting | bytes 20643840 | tf_op jit(solution)/shard_map/reshape | solution.py:153
  415.5 13.9 %all_to_all.22 = bf16[2,64,14,2880]{3,1,2,0:T(8,128)(2,1)} all-to-all(bf16[2,64,14,2880]{3,1,2,0:T(8,128)(2,1)S(1)} %copy.132), channel_id=1, replica_groups=mesh['req'=16,'y'=4,'c'=2] {'c'}, dimensions={0} | all-to-all | bytes 20643840 | tf_op jit(solution)/shard_map/all_to_all | solution.py:152
  429.5 9.7 %reduce_sum.105 = bf16[64,14,2880]{2,0,1:T(8,128)(2,1)} reduce(bf16[2,64,14,2880]{3,1,2,0:T(8,128)(2,1)} %all_to_all.22, bf16[]{:T(256)} %constant.70.clone.1), dimensions={0}, to_apply=%region_14.15 | reduce | flops 2580480 | bytes 15482882 | tf_op jit(solution)/shard_map/reduce_sum | solution.py:155
  439.1 8.0 %copy.133 = bf16[64,14,2880]{2,1,0:T(8,128)(2,1)} copy(bf16[64,14,2880]{2,0,1:T(8,128)(2,1)} %reduce_sum.105) | data formatting | bytes 10321920 | tf_op jit(solution)/shard_map/reduce_sum | solution.py:155
  447.1 11.1 %all-to-all-start.3 = ((bf16[64,14,2880]{2,1,0:T(8,128)(2,1)}), bf16[64,14,2880]{2,1,0:T(8,128)(2,1)}, u32[]{:S(2)}, u32[]{:S(2)}) async-start(bf16[64,14,2880]{2,1,0:T(8,128)(2,1)} %copy.133), calls=%async_computation.4 | async-start | bytes 12058624 | tf_op jit(solution)/shard_map/all_to_all | solution.py:156
  463.2 76.9 %all-to-all-done.3 = bf16[64,14,2880]{2,1,0:T(8,128)(2,1)} async-done(((bf16[64,14,2880]{2,1,0:T(8,128)(2,1)}), bf16[64,14,2880]{2,1,0:T(8,128)(2,1)}, u32[]{:S(2)}, u32[]{:S(2)}) %all-to-all-start.3) | async-done | bytes 5160992 | tf_op jit(solution)/shard_map/all_to_all | solution.py:156
  540.1 7.0 %convert_reduce_fusion = f32[32,14,2880]{2,1,0:T(8,128)} fusion(bf16[64,14,2880]{2,1,0:T(8,128)(2,1)} %all-to-all-done.3), kind=kLoop, calls=%fused_computation.9 | loop fusion | flops 3870720 | bytes 10321920 | tf_op jit(solution)/shard_map/reduce_sum | solution.py:157
  552.8 9.0 %gather_fusion = f32[384,2880]{1,0:T(8,128)} fusion(f32[448,2880]{1,0:T(8,128)} %reshape.436, s32[1024]{0:T(1024)S(1)} %pad_clamp_fusion), kind=kCustom, calls=%fused_computation | custom fusion | bytes 8848896 | tf_op jit(solution)/shard_map/jit(_take)/gather | solution.py:159
  (104 shorter events, 78.0 us)
Async XLA Ops:
  6.5 90.3 %copy-start = (bf16[512,2880]{0,1:T(8,128)(2,1)S(1)}, bf16[512,2880]{0,1:T(8,128)(2,1)}, u32[]{:S(2)}) copy-start(bf16[512,2880]{0,1:T(8,128)(2,1)} %param.20) | copy-start | bytes 8847364
  6.5 8.2 %copy-start.14 = (s32[1,6]{1,0:T(1,128)S(1)}, s32[1,6]{1,0:T(1,128)}, u32[]{:S(2)}) copy-start(s32[1,6]{1,0:T(1,128)} %param.24) | copy-start | bytes 76
  6.5 37.2 %all-gather.5.cloned.1.call-start = ((), (), s32[]{:S(2)}) async-start(), calls=%async_computation.6 | async-start | bytes 2826240 | tf_op jit(solution)/shard_map/all_gather | solution.py:64
  10.1 134.6 %all-reduce.3.cloned.1.call-start = ((), (), s32[]{:S(2)}) async-start(), calls=%async_computation.8 | async-start | bytes 9043968
  54.1 1.0 copy-start.8
  54.4 6.2 %copy-start.2 = (bf16[4,2,96,2880]{3,2,1,0:T(8,128)(2,1)}, bf16[4,2,96,2880]{3,2,1,0:T(8,128)(2,1)S(1)}, u32[]{:S(2)}) copy-start(bf16[4,2,96,2880]{3,2,1,0:T(8,128)(2,1)S(1)} %copy.116) | copy-start | bytes 13271044
  54.4 3.5 copy-start.5
  58.0 2.7 copy-start.6
  58.0 2.7 copy-start.7
  60.9 8.8 %copy-start.13 = (f32[8]{0:T(128)S(1)}, f32[8]{0:T(128)}, u32[]{:S(2)}) copy-start(f32[8]{0:T(128)} %param.19) | copy-start | bytes 100
  69.0 0.6 copy-start.9
  102.5 6.7 %copy-start.15 = (u32[128]{0:T(128)S(1)}, u32[128]{0:T(128)}, u32[]{:S(2)}) copy-start(u32[128]{0:T(128)} %constant.92) | copy-start | bytes 1540
  109.1 39.5 %copy-start.11 = (s32[96,4]{0,1:T(4,128)S(1)}, s32[96,4]{0,1:T(4,128)}, u32[]{:S(2)}) copy-start(s32[96,4]{0,1:T(4,128)} %param.23) | copy-start | bytes 4612
  109.1 70.7 %copy-start.3 = (bf16[96,2880]{1,0:T(8,128)(2,1)S(1)}, bf16[96,2880]{1,0:T(8,128)(2,1)}, u32[]{:S(2)}) copy-start(bf16[96,2880]{1,0:T(8,128)(2,1)} %param.14) | copy-start | bytes 1658884
  109.1 72.0 %copy-start.12 = (f32[2880]{0:T(1024)S(1)}, f32[2880]{0:T(1024)}, u32[]{:S(2)}) copy-start(f32[2880]{0:T(1024)} %param.21) | copy-start | bytes 34564
  109.2 70.7 %reduce-scatter.3.cloned.1.call-start = ((), (), s32[]{:S(2)}) async-start(), calls=%async_computation.5 | async-start | bytes 2826240 | tf_op jit(solution)/shard_map/reduce_scatter | solution.py:116
  148.6 156.1 %all-gather.7.cloned.1.call-start = ((), (), s32[]{:S(2)}) async-start(), calls=%async_computation.7 | async-start | bytes 15826944 | tf_op jit(solution)/shard_map/all_gather | solution.py:144
  447.1 11.9 %copy-start.10 = (bf16[2880,32]{0,1:T(8,128)(2,1)S(1)}, bf16[2880,32]{0,1:T(8,128)(2,1)}, u32[]{:S(2)}) copy-start(bf16[2880,32]{0,1:T(8,128)(2,1)} %param.22) | copy-start | bytes 552964
  447.1 92.9 %all-to-all-start.3 = ((bf16[64,14,2880]{2,1,0:T(8,128)(2,1)}), bf16[64,14,2880]{2,1,0:T(8,128)(2,1)}, u32[]{:S(2)}, u32[]{:S(2)}) async-start(bf16[64,14,2880]{2,1,0:T(8,128)(2,1)} %copy.133), calls=%async_computation.4 | async-start | bytes 12058624 | tf_op jit(solution)/shard_map/all_to_all | solution.py:156
  561.8 13.1 %copy-start.1 = (bf16[512,2880]{0,1:T(8,128)(2,1)S(1)}, bf16[512,2880]{0,1:T(8,128)(2,1)}, u32[]{:S(2)}) copy-start(bf16[512,2880]{0,1:T(8,128)(2,1)} %param.20) | copy-start | bytes 8847364
  567.3 6.5 %copy-start.4 = (bf16[1,96,2880]{2,1,0:T(8,128)(2,1)S(1)}, bf16[1,96,2880]{2,1,0:T(8,128)(2,1)}, u32[]{:S(2)}) copy-start(bf16[1,96,2880]{2,1,0:T(8,128)(2,1)} %reduce-scatter.3.cloned.1.call-done) | copy-start | bytes 1658884
Sparse Core Ops, SparseCore 0:
  10.2 33.5 all-gather.4
  109.2 35.4 all-reduce.2
  148.7 31.0 reduce-scatter.2
  280.7 23.9 all-gather.6
